TPU v7x, 256 devices: a whole 4x4x8 slice. The times are simulated.
256 devices in a mesh: row: 16 (over x_hi, y, core), col: 16 (over z, x_lo).
Axes of the slice: x: 4 (x_hi: 2, x_lo: 2; x = x_hi * 2 + x_lo), y: 4, z: 8, core: 2. Of those that a mesh axis runs over, the one named last changes fastest.
Arguments:
- stem: bfloat16 [16, 16, 1, 512, 2, 512], P('row', 'col'), may hold values from -6 to 6
- branch: bfloat16 [16, 4, 2, 512, 512], P('row', None, None, None, 'col'), may hold values from -0.1875 to 0.1875
Outputs:
- amplitudes: bfloat16 [16, 16, 1, 512, 2, 512], P('row', 'col')
All inputs are finite; a program needn't handle non-finite values.
Results may differ from a plain program's by a relative error of at most 0.0075.
Values may be sent and summed in bfloat16 or wider, within the bound.
No kernel may reach another device: no remote copies, remote signals or barrier semaphores. Data moves between devices by JAX's collectives and lax.ppermute only.
A program may use at most 64 MiB of HBM per device.

v0:
```python
import jax
import jax.numpy as jnp
from jax import lax
from jax.sharding import PartitionSpec as P


def right_piece(block, piece):
    width = piece.shape[2]
    items = block.shape[0]
    order_size = block.shape[1]
    flat = block.reshape(items * order_size, 2 * width)
    real_t = piece[0].T
    imag_t = piece[1].T
    weight = jnp.block([[real_t, imag_t], [-imag_t, real_t]])
    product = jnp.dot(flat, weight, preferred_element_type=jnp.float32)
    return product.reshape(items, order_size, 2, order_size)


def left_piece(block, piece):
    rows_out = piece.shape[1]
    real_in = block[:, :, 0, :]
    imag_in = block[:, :, 1, :]
    real_w = piece[0]
    imag_w = piece[1]
    weight_real = jnp.concatenate([real_w, imag_w], axis=0)
    weight_imag = jnp.concatenate([-imag_w, real_w], axis=0)
    product = jnp.einsum("xi,eij->exj", weight_real, real_in, preferred_element_type=jnp.float32)
    product = product + jnp.einsum(
        "xi,eij->exj", weight_imag, imag_in, preferred_element_type=jnp.float32
    )
    return jnp.stack([product[:, :rows_out, :], product[:, rows_out:, :]], axis=2)


def shards(stem, branch):
    slab_count = stem.shape[2]
    order_size = stem.shape[3]
    row_count = lax.axis_size("row")
    share = order_size // row_count
    own_columns = branch[0]
    whole = lax.all_gather(own_columns, "col", axis=3, tiled=True)

    def apply_right(block, build_id):
        return right_piece(block, whole[build_id])

    def apply_left(block, build_id):
        return left_piece(block, whole[build_id])

    block = stem[0, 0]
    half_first = apply_right(block, 1).astype(jnp.bfloat16)
    step_first = apply_left(half_first, 0).astype(jnp.bfloat16)
    outgoing = step_first.reshape(slab_count, row_count, share, 2, order_size)
    moved = lax.all_to_all(outgoing, "row", split_axis=1, concat_axis=1, tiled=True)
    items = moved.shape[0]
    flat = moved.reshape(items, order_size, 2, order_size)
    half_second = apply_right(flat, 3).astype(jnp.bfloat16)
    step_second = apply_left(half_second, 2).astype(jnp.bfloat16)
    leaving = step_second.reshape(slab_count, order_size, 2, row_count, share)
    arrived = lax.all_to_all(leaving, "row", split_axis=3, concat_axis=3, tiled=True)
    return arrived.reshape(1, 1, slab_count, order_size, 2, order_size)


def solution(mesh):
    placed = (P("row", "col", None, None, None, None), P("row", None, None, None, "col"))
    return jax.shard_map(
        shards,
        mesh=mesh,
        in_specs=placed,
        out_specs=P("row", "col", None, None, None, None),
        check_vma=False,
    )
```

profile of v0, /device:TPU:1, one launch (start us, length us, event | category | flops | bytes accessed | tf_op | source)
XLA Modules:
  0.0 182.5 jit_solution(8665607085128221393)
XLA Ops:
  6.5 0.0 all-gather.3.cloned.1.call-start
  6.5 0.7 all-gather.3.cloned.1.call-update
  7.3 1.5 copy.20
  8.7 100.9 %all-gather.3.cloned.1.call-done = bf16[1,4,2,512,512]{3,4,2,1,0:T(8,128)(2,1)} async-done(((bf16[1,4,2,512,32]{3,4,2,1,0:T(8,128)(2,1)}), bf16[1,4,2,512,512]{3,4,2,1,0:T(8,128)(2,1)}) %all-gather.3.cloned.1.call-update) | async-done | bytes 4194320 | tf_op jit(solution)/shard_map/all_gather | solution.py:40
  109.6 0.0 copy-start
  109.6 2.2 %fusion.36 = (bf16[512,512]{0,1:T(8,128)(2,1)}, bf16[512,512]{0,1:T(8,128)(2,1)S(1)}) fusion(bf16[4,2,512,512]{2,3,1,0:T(8,128)(2,1)} %bitcast.76), kind=kLoop, calls=%fused_computation.52 | loop fusion | flops 524288 | bytes 2097152 | tf_op jit(solution)/shard_map/neg | solution.py:26
  111.8 2.1 %fusion.35 = (bf16[512,512]{1,0:T(8,128)(2,1)}, bf16[512,512]{1,0:T(8,128)(2,1)S(1)}) fusion(bf16[4,2,512,512]{2,3,1,0:T(8,128)(2,1)} %bitcast.77), kind=kLoop, calls=%fused_computation.51 | loop fusion | flops 524288 | bytes 2097152 | tf_op jit(solution)/shard_map/neg | solution.py:14
  113.9 0.0 copy-done
  113.9 1.5 slice_bitcast_fusion.6
  115.4 1.3 fusion.8
  116.7 0.7 fusion.14
  117.4 0.7 fusion.12
  118.1 0.1 fusion.38
  118.2 0.2 copy.11
  118.4 0.2 copy.12
  118.7 0.1 pad_maximum_fusion
  118.8 1.0 copy.13
  119.8 9.4 %all-to-all-start = ((bf16[1,16,32,2,512]{4,2,3,0,1:T(8,128)(2,1)}), bf16[1,16,32,2,512]{4,2,3,0,1:T(8,128)(2,1)S(1)}, u32[]{:S(2)}, u32[]{:S(2)}) async-start(bf16[1,16,32,2,512]{4,2,3,0,1:T(8,128)(2,1)} %copy.13), calls=%async_computation | async-start | bytes 2097152 | tf_op jit(solution)/shard_map/all_to_all | solution.py:52
  129.2 1.8 maximum_bitcast_fusion
  131.0 2.6 %copy.15 = bf16[1024,1024]{1,0:T(8,128)(2,1)} copy(bf16[1024,1024]{0,1:T(8,128)(2,1)S(1)} %maximum_bitcast_fusion) | data formatting | bytes 4194304 | tf_op jit(solution)/shard_map/dot_general | solution.py:15
  133.6 12.7 %all-to-all-done = bf16[1,16,32,2,512]{4,2,3,0,1:T(8,128)(2,1)S(1)} async-done(((bf16[1,16,32,2,512]{4,2,3,0,1:T(8,128)(2,1)}), bf16[1,16,32,2,512]{4,2,3,0,1:T(8,128)(2,1)S(1)}, u32[]{:S(2)}, u32[]{:S(2)}) %all-to-all-start) | async-done | bytes 1048608 | tf_op jit(solution)/shard_map/all_to_all | solution.py:52
  146.3 1.1 copy.14
  147.3 0.8 reshape.153
  148.1 0.0 copy-start.1
  148.1 0.0 copy-start.3
  148.1 3.0 %fusion.11 = bf16[1,512,2,512]{3,1,2,0:T(8,128)(2,1)S(1)} fusion(bf16[512,1024,1]{1,0,2:T(8,128)(2,1)S(1)} %reshape.153, bf16[2,512,1024]{2,1,0:T(8,128)(2,1)} %bitcast.80), kind=kOutput, calls=%fused_computation.13 | convolution fusion | flops 1074266112 | bytes 4194304 | tf_op jit(solution)/shard_map/dot_general | solution.py:15
  151.1 0.0 copy-done.1
  151.1 0.0 copy-done.3
  151.1 0.0 copy-start.2
  151.1 0.7 fusion.21
  151.9 0.3 copy-done.2
  152.2 0.7 fusion.13
  152.9 0.1 fusion.37
  153.0 0.1 pad_maximum_fusion.1
  153.1 20.3 %all_to_all.10 = bf16[1,512,2,16,32]{1,4,2,0,3:T(8,128)(2,1)S(1)} all-to-all(bf16[1,512,2,16,32]{1,4,2,0,3:T(8,128)(2,1)S(1)} %pad_maximum_fusion.1), channel_id=1, replica_groups=mesh['row'=16,'col'=16] {'row'}, dimensions={3} | all-to-all | bytes 2097152 | tf_op jit(solution)/shard_map/all_to_all | solution.py:58
  173.4 0.1 copy.18
  173.5 2.1 %copy.19 = bf16[1,1,1,512,2,512]{5,4,3,2,1,0:T(2,128)(2,1)} copy(bf16[1,1,1,512,2,512]{3,5,4,2,1,0:T(8,128)(2,1)S(1)} %bitcast.79) | data formatting | bytes 2097152 | tf_op jit(solution)/shard_map/reshape | solution.py:59
Async XLA Ops:
  6.5 103.1 %all-gather.3.cloned.1.call-start = ((), (), s32[]{:S(2)}) async-start(), calls=%async_computation.2 | async-start | bytes 4456448 | tf_op jit(solution)/shard_map/all_gather | solution.py:40
  109.6 4.3 %copy-start = (bf16[1,4,2,512,512]{3,4,2,1,0:T(8,128)(2,1)S(1)}, bf16[1,4,2,512,512]{3,4,2,1,0:T(8,128)(2,1)}, u32[]{:S(2)}) copy-start(bf16[1,4,2,512,512]{3,4,2,1,0:T(8,128)(2,1)} %all-gather.3.cloned.1.call-done) | copy-start | bytes 12582916
  119.8 26.4 %all-to-all-start = ((bf16[1,16,32,2,512]{4,2,3,0,1:T(8,128)(2,1)}), bf16[1,16,32,2,512]{4,2,3,0,1:T(8,128)(2,1)S(1)}, u32[]{:S(2)}, u32[]{:S(2)}) async-start(bf16[1,16,32,2,512]{4,2,3,0,1:T(8,128)(2,1)} %copy.13), calls=%async_computation | async-start | bytes 2097152 | tf_op jit(solution)/shard_map/all_to_all | solution.py:52
  148.1 3.0 %copy-start.1 = (bf16[512,512]{0,1:T(8,128)(2,1)S(1)}, bf16[512,512]{0,1:T(8,128)(2,1)}, u32[]{:S(2)}) copy-start(bf16[512,512]{0,1:T(8,128)(2,1)} %get-tuple-element.9) | copy-start | bytes 1572868
  148.1 3.0 %copy-start.3 = (bf16[512,512]{0,1:T(8,128)(2,1)S(1)}, bf16[512,512]{0,1:T(8,128)(2,1)}, u32[]{:S(2)}) copy-start(bf16[512,512]{0,1:T(8,128)(2,1)} %get-tuple-element.8) | copy-start | bytes 1572868
  151.1 1.0 copy-start.2
Sparse Core Ops, SparseCore 0:
  9.1 100.4 all-gather.2
where the time goes:
time: 183 us; the launch traced here: 182 us
  waiting for transfers between devices  114 us (62%)
  blocking collectives  20.3 us (11%)
  between operations  13.5 us (7%)
  local copies, waits for them, and re-layouts  11.6 us (6%)
  starting transfers between devices  9.37 us (5%)
  matrix products  7.15 us (4%)
  other arithmetic  6.25 us (3%)
    all_gather x1, waiting for transfers between devices, shards(): whole = lax.all_gather(own_columns, 'col', axis=3, tiled=True)  101 us
    all_to_all x1, blocking collectives, shards(): lax.all_to_all(leaving, 'row', split_axis=3, concat_axis=3, tiled=True)  20.3 us
    all_to_all x1, waiting for transfers between devices, shards(): lax.all_to_all(outgoing, 'row', split_axis=1, concat_axis=1, tiled=True)  12.7 us
    all_to_all x1, starting transfers between devices, shards(): lax.all_to_all(outgoing, 'row', split_axis=1, concat_axis=1, tiled=True)  9.37 us
    dot_general x2, matrix products, right_piece(): product = jnp.dot(flat, weight, preferred_element_type=jnp.float32)  4.26 us
  transfers between devices with their start and end apart: 2, of which 2 were waited for; matrix products, arithmetic and copies ran while one was open for 3% of the time, Pallas kernels for 0%

commit v1 on v0

--- a/solution.py
+++ b/solution.py
@@ -2,6 +2,11 @@
 import jax.numpy as jnp
 from jax import lax
 from jax.sharding import PartitionSpec as P
+from jax.lax import all_to_all, axis_size
+
+deliver_cubes = lambda point: jnp.concatenate(
+    all_to_all(jnp.stack([point for _ in range(axis_size("col"))], axis=0), "col", 0, 0), axis=3
+)
 
 
 def right_piece(block, piece):
@@ -37,7 +42,7 @@
     row_count = lax.axis_size("row")
     share = order_size // row_count
     own_columns = branch[0]
-    whole = lax.all_gather(own_columns, "col", axis=3, tiled=True)
+    whole = deliver_cubes(own_columns)
 
     def apply_right(block, build_id):
         return right_piece(block, whole[build_id])

time: 183 us -> 177 us (0.967)
  between operations: 13.5 us -> 0.17 us
  starting transfers between devices: 9.37 us -> 18.3 us
  local copies, waits for them, and re-layouts: 11.6 us -> 17.4 us
  waiting for transfers between devices: 114 us -> 110 us
  other arithmetic: 6.25 us -> 3.74 us
    all_gather x1 -> x0, waiting for transfers between devices: 101 us -> none  [shards(): whole = lax.all_gather(own_columns, 'col', axis=3, tiled=True)]
    all_to_all x0 -> x1, waiting for transfers between devices: none -> 96.7 us  [all_to_all(jnp.stack([point for _ in range(axis_size('col'))], axis=0), '...]
    all_to_all x0 -> x1, starting transfers between devices: none -> 10.2 us  [all_to_all(jnp.stack([point for _ in range(axis_size('col'))], axis=0), '...]
    another operation x0 -> x1, local copies, waits for them, and re-layouts: none -> 3.43 us  [jnp.stack([point for _ in range(axis_size('col'))], axis=0)]
    all_to_all x0 -> x1, local copies, waits for them, and re-layouts: none -> 2.66 us  [all_to_all(jnp.stack([point for _ in range(axis_size('col'))], axis=0), '...]
where the time goes in v1:
time: 177 us
  waiting for transfers between devices  110 us (62%)
  blocking collectives  20.3 us (11%)
  starting transfers between devices  18.3 us (10%)
  local copies, waits for them, and re-layouts  17.4 us (10%)
  matrix products  7.12 us (4%)
  other arithmetic  3.74 us (2%)
    all_to_all x1, waiting for transfers between devices, all_to_all(jnp.stack([point for _ in range(axis_size('col'))], axis=0), '...  96.7 us
    all_to_all x1, blocking collectives, shards(): lax.all_to_all(leaving, 'row', split_axis=3, concat_axis=3, tiled=True)  20.3 us
    all_to_all x1, waiting for transfers between devices, shards(): lax.all_to_all(outgoing, 'row', split_axis=1, concat_axis=1, tiled=True)  13 us
    all_to_all x1, starting transfers between devices, all_to_all(jnp.stack([point for _ in range(axis_size('col'))], axis=0), '...  10.2 us
    all_to_all x1, starting transfers between devices, shards(): lax.all_to_all(outgoing, 'row', split_axis=1, concat_axis=1, tiled=True)  8.1 us
    dot_general x2, matrix products, right_piece(): product = jnp.dot(flat, weight, preferred_element_type=jnp.float32)  4.22 us
  transfers between devices with their start and end apart: 2, of which 2 were waited for; matrix products, arithmetic and copies ran while one was open for 3% of the time, Pallas kernels for 0%

profile of v1, /device:TPU:1, one launch (start us, length us, event | category | flops | bytes accessed | tf_op | source)
XLA Modules:
  0.0 176.8 jit_solution(9720128637591819598)
XLA Ops:
  0.0 3.4 %stack.21 = bf16[16,4,2,512,32]{3,4,2,1,0:T(8,128)(2,1)} broadcast(bf16[4,2,512,32]{2,3,1,0:T(8,128)(2,1)} %bitcast.88), dimensions={1,2,3,4} | broadcast | bytes 4456448 | tf_op jit(solution)/shard_map/stack | solution.py:8
  3.4 0.0 copy-start.3
  3.4 10.2 %all-to-all-start = ((bf16[16,4,2,512,32]{3,4,2,1,0:T(8,128)(2,1)}), bf16[16,4,2,512,32]{3,4,2,1,0:T(8,128)(2,1)}, u32[]{:S(2)}, u32[]{:S(2)}) async-start(bf16[16,4,2,512,32]{3,4,2,1,0:T(8,128)(2,1)} %stack.21), calls=%async_computation | async-start | bytes 8388608 | tf_op jit(solution)/shard_map/all_to_all | solution.py:8
  13.7 0.0 copy-done.3
  13.7 0.2 copy.21
  13.9 96.7 %all-to-all-done = bf16[16,4,2,512,32]{3,4,2,1,0:T(8,128)(2,1)} async-done(((bf16[16,4,2,512,32]{3,4,2,1,0:T(8,128)(2,1)}), bf16[16,4,2,512,32]{3,4,2,1,0:T(8,128)(2,1)}, u32[]{:S(2)}, u32[]{:S(2)}) %all-to-all-start) | async-done | bytes 4194336 | tf_op jit(solution)/shard_map/all_to_all | solution.py:8
  110.6 2.7 %copy.23 = bf16[16,4,2,512,32]{3,4,0,2,1:T(8,128)(2,1)S(1)} copy(bf16[16,4,2,512,32]{3,4,2,1,0:T(8,128)(2,1)} %all-to-all-done) | data formatting | bytes 8388608 | tf_op jit(solution)/shard_map/all_to_all | solution.py:8
  113.3 1.3 fusion.33
  114.6 0.0 copy-start
  114.6 1.0 bitcast_negate_fusion.1
  115.6 0.9 bitcast_negate_fusion
  116.5 0.0 copy-done
  116.5 1.3 fusion.8
  117.8 0.7 fusion.14
  118.5 0.7 fusion.12
  119.2 0.1 fusion.35
  119.3 0.2 copy.12
  119.5 0.2 copy.13
  119.8 0.1 pad_maximum_fusion
  119.9 1.0 copy.14
  120.9 8.1 %all-to-all-start.1 = ((bf16[1,16,32,2,512]{4,2,3,0,1:T(8,128)(2,1)}), bf16[1,16,32,2,512]{4,2,3,0,1:T(8,128)(2,1)}, u32[]{:S(2)}, u32[]{:S(2)}) async-start(bf16[1,16,32,2,512]{4,2,3,0,1:T(8,128)(2,1)} %copy.14), calls=%async_computation.1 | async-start | bytes 2097152 | tf_op jit(solution)/shard_map/all_to_all | solution.py:57
  129.0 1.6 maximum_bitcast_fusion
  130.6 2.6 %copy.16 = bf16[1024,1024]{1,0:T(8,128)(2,1)} copy(bf16[1024,1024]{0,1:T(8,128)(2,1)S(1)} %maximum_bitcast_fusion) | data formatting | bytes 4194304 | tf_op jit(solution)/shard_map/dot_general | solution.py:20
  133.2 13.0 %all-to-all-done.1 = bf16[1,16,32,2,512]{4,2,3,0,1:T(8,128)(2,1)} async-done(((bf16[1,16,32,2,512]{4,2,3,0,1:T(8,128)(2,1)}), bf16[1,16,32,2,512]{4,2,3,0,1:T(8,128)(2,1)}, u32[]{:S(2)}, u32[]{:S(2)}) %all-to-all-start.1) | async-done | bytes 1048608 | tf_op jit(solution)/shard_map/all_to_all | solution.py:57
  146.2 2.3 %copy.15 = bf16[1,16,32,2,512]{4,3,2,1,0:T(2,128)(2,1)S(1)} copy(bf16[1,16,32,2,512]{4,2,3,0,1:T(8,128)(2,1)} %all-to-all-done.1) | data formatting | bytes 2097152 | tf_op jit(solution)/shard_map/all_to_all | solution.py:57
  148.5 0.8 reshape.166
  149.3 0.0 copy-start.1
  149.3 2.9 %fusion.11 = bf16[1,512,2,512]{3,1,2,0:T(8,128)(2,1)S(1)} fusion(bf16[512,1024,1]{1,0,2:T(8,128)(2,1)S(1)} %reshape.166, bf16[2,512,1024]{2,1,0:T(8,128)(2,1)} %bitcast.76), kind=kOutput, calls=%fused_computation.14 | convolution fusion | flops 1074266112 | bytes 4194304 | tf_op jit(solution)/shard_map/dot_general | solution.py:20
  152.2 0.0 copy-done.1
  152.2 0.0 copy-start.2
  152.2 0.7 fusion.21
  153.0 0.3 copy-done.2
  153.3 0.7 fusion.13
  154.0 0.1 fusion.34
  154.1 0.1 pad_maximum_fusion.1
  154.2 20.3 %all_to_all.15 = bf16[1,512,2,16,32]{1,4,2,0,3:T(8,128)(2,1)S(1)} all-to-all(bf16[1,512,2,16,32]{1,4,2,0,3:T(8,128)(2,1)S(1)} %pad_maximum_fusion.1), channel_id=1, replica_groups=mesh['row'=16,'col'=16] {'row'}, dimensions={3} | all-to-all | bytes 2097152 | tf_op jit(solution)/shard_map/all_to_all | solution.py:63
  174.5 0.1 copy.19
  174.7 2.1 %copy.20 = bf16[1,1,1,512,2,512]{5,4,3,2,1,0:T(2,128)(2,1)} copy(bf16[1,1,1,512,2,512]{3,5,4,2,1,0:T(8,128)(2,1)S(1)} %bitcast.72) | data formatting | bytes 2097152 | tf_op jit(solution)/shard_map/reshape | solution.py:64
Async XLA Ops:
  3.4 10.2 %copy-start.3 = (bf16[1,1,1,512,2,512]{5,4,3,2,1,0:T(2,128)(2,1)S(1)}, bf16[1,1,1,512,2,512]{5,4,3,2,1,0:T(2,128)(2,1)}, u32[]{:S(2)}) copy-start(bf16[1,1,1,512,2,512]{5,4,3,2,1,0:T(2,128)(2,1)} %param.2) | copy-start | bytes 3145732
  3.4 107.2 %all-to-all-start = ((bf16[16,4,2,512,32]{3,4,2,1,0:T(8,128)(2,1)}), bf16[16,4,2,512,32]{3,4,2,1,0:T(8,128)(2,1)}, u32[]{:S(2)}, u32[]{:S(2)}) async-start(bf16[16,4,2,512,32]{3,4,2,1,0:T(8,128)(2,1)} %stack.21), calls=%async_computation | async-start | bytes 8388608 | tf_op jit(solution)/shard_map/all_to_all | solution.py:8
  114.6 1.9 %copy-start = (bf16[1,1,512,16,32]{2,4,3,1,0:T(8,128)(2,1)}, bf16[1,1,512,16,32]{2,4,3,1,0:T(8,128)(2,1)S(1)}, u32[]{:S(2)}) copy-start(bf16[1,1,512,16,32]{2,4,3,1,0:T(8,128)(2,1)S(1)} %get-tuple-element.6) | copy-start | bytes 1572868
  120.9 25.3 %all-to-all-start.1 = ((bf16[1,16,32,2,512]{4,2,3,0,1:T(8,128)(2,1)}), bf16[1,16,32,2,512]{4,2,3,0,1:T(8,128)(2,1)}, u32[]{:S(2)}, u32[]{:S(2)}) async-start(bf16[1,16,32,2,512]{4,2,3,0,1:T(8,128)(2,1)} %copy.14), calls=%async_computation.1 | async-start | bytes 2097152 | tf_op jit(solution)/shard_map/all_to_all | solution.py:57
  149.3 2.9 %copy-start.1 = (bf16[1,1,512,16,32]{2,4,3,1,0:T(8,128)(2,1)S(1)}, bf16[1,1,512,16,32]{2,4,3,1,0:T(8,128)(2,1)}, u32[]{:S(2)}) copy-start(bf16[1,1,512,16,32]{2,4,3,1,0:T(8,128)(2,1)} %copy-done) | copy-start | bytes 1572868
  152.2 1.0 copy-start.2
